TPU v7x, 128 devices: a whole 4x4x4 slice. The times are simulated.
128 devices in a mesh: row: 16 (over z_lo, x, core), col: 8 (over y, z_hi).
Axes of the slice: x: 4, y: 4, z: 4 (z_hi: 2, z_lo: 2; z = z_hi * 2 + z_lo), core: 2. Of those that a mesh axis runs over, the one named last changes fastest.
Arguments:
- shared_rows: float32 [2048, 16384], P('row', 'col'), may hold values from -0.125 to 0.125
- event_counts: int32 [16], replicated, may hold values from 32 to 128, as said below
- ridge: float32 [16384], P('col'), may hold values from 0.5 to 2
- items: float32 [1024, 16384], P('row', 'col'), may hold values from -6 to 6
- cand_ids: int32 [512], replicated, may hold values from 0 to 1023
- theta: float32 [16384], P('col'), may hold values from -0.046875 to 0.046875
Outputs:
- gram_tile: float32 [16384, 16384], P('row', 'col')
- scores: float32 [512], replicated
Inputs may be any that keep to these rules, and one draw needn't show every extreme that they name: event_counts[s] counts the live slots at the start of row shard s's 128 slots; some shard is full.
All inputs are finite; a program needn't handle non-finite values.
Results may differ from a plain program's by a relative error of at most 0.000068.
Values sent between devices are 32-bit elements; how exact they have to be, the bound alone decides.
No kernel may reach another device: no remote copies, remote signals or barrier semaphores. Data moves between devices by JAX's collectives and lax.ppermute only.
A program may use at most 128 MiB of HBM per device.

v0:
```python
import jax
import jax.numpy as jnp
from jax import lax
from jax.sharding import PartitionSpec as P

F = 16384
high = lax.Precision.HIGHEST


def spread(value, axis, source):
    kept = jnp.where(lax.axis_index(axis) == source, value, 0).astype(value.dtype)
    return lax.psum(kept, axis)


def body(shared_rows, event_counts, ridge, items, cand_ids, theta):
    ratio = lax.axis_size("row") // lax.axis_size("col")
    row_pos = lax.axis_index("row")
    col_pos = lax.axis_index("col")
    width_col = shared_rows.shape[1]
    width_row = width_col // ratio
    ev_slots = shared_rows.shape[0]
    slot = lax.iota(jnp.int32, ev_slots)
    masked = jnp.where((slot < event_counts[row_pos])[:, None], shared_rows, jnp.float32(0.0))
    offset = row_pos % ratio * width_row
    root = row_pos // ratio
    contract = (((0,), (0,)), ((), ()))
    col_all = lax.all_gather(masked, "row", axis=0, tiled=True)
    row_all = spread(lax.dynamic_slice_in_dim(col_all, offset, width_row, 1), "col", root)
    tile = lax.dot_general(
        row_all, col_all, contract, precision=high, preferred_element_type=jnp.float32
    )
    rows_global = row_pos * width_row + lax.broadcasted_iota(jnp.int32, (width_row, width_col), 0)
    cols_global = col_pos * width_col + lax.broadcasted_iota(jnp.int32, (width_row, width_col), 1)
    tile = tile + jnp.where(rows_global == cols_global, ridge[None, :], jnp.float32(0.0))
    items_dev = items.shape[0]
    onehot = (
        cand_ids[:, None] == row_pos * items_dev + lax.iota(jnp.int32, items_dev)[None, :]
    ).astype(jnp.float32)
    picked = jnp.dot(onehot, items, precision=high, preferred_element_type=jnp.float32)
    cand_col = lax.psum(picked, "row")
    across = (((1,), (1,)), ((), ()))
    cand_row = spread(lax.dynamic_slice_in_dim(cand_col, offset, width_row, 1), "col", root)
    image_part = lax.dot_general(
        cand_col, tile, across, precision=high, preferred_element_type=jnp.float32
    )
    image_row = lax.psum(image_part, "col")
    quad = jnp.where(col_pos == 0, jnp.sum(cand_row * image_row, axis=1), jnp.float32(0.0))
    linear = jnp.where(
        row_pos == 0,
        jnp.dot(cand_col, theta, precision=high, preferred_element_type=jnp.float32),
        jnp.float32(0.0),
    )
    quad_all, linear_all = lax.psum((quad, linear), ("row", "col"))
    return (tile, linear_all + jnp.sqrt(quad_all / F))


def solution(mesh):
    return jax.shard_map(
        body,
        mesh=mesh,
        in_specs=(P("row", "col"), P(), P("col"), P("row", "col"), P(), P("col")),
        out_specs=(P("row", "col"), P()),
        check_vma=False,
    )
```

profile of v0, /device:TPU:1, one launch (start us, length us, event | category | flops | bytes accessed | tf_op | source)
XLA Modules:
  0.0 940.3 jit_solution(5957106584917055528)
XLA Ops:
  7.2 0.0 copy-start
  7.2 0.0 all-gather.2.cloned.1.call-start
  7.2 1.3 dynamic_slice.9
  8.5 0.6 iota_compare_fusion
  9.2 2.3 broadcast_select_fusion
  11.5 0.0 all-gather.2.cloned.1.call-update
  11.5 0.0 all-reduce.8.cloned.1.call-start
  11.6 0.0 copy-done
  11.6 4.5 fusion
  16.1 0.0 all-reduce.8.cloned.1.call-update
  16.1 0.0 all-reduce.6.cloned.1.call-start
  16.2 90.8 %all-gather.2.cloned.1.call-done = f32[2048,2048]{1,0:T(8,128)} async-done(((f32[128,2048]{1,0:T(8,128)}), f32[2048,2048]{1,0:T(8,128)}) %all-gather.2.cloned.1.call-update) | async-done | bytes 16777232 | tf_op jit(solution)/shard_map/all_gather | solution.py:27
  107.0 8.7 dynamic-slice_select_fusion
  115.7 0.0 copy-start.3
  115.7 0.0 all-reduce.6.cloned.1.call-update
  115.7 0.0 all-reduce.10.cloned.1.call-start
  115.8 122.9 %all-reduce.8.cloned.1.call-done = f32[512,2048]{1,0:T(8,128)} async-done(((f32[512,2048]{1,0:T(8,128)}), f32[512,2048]{1,0:T(8,128)}) %all-reduce.8.cloned.1.call-update) | async-done | bytes 4194320 | tf_op jit(solution)/shard_map/psum | solution.py:40
  238.7 3.2 dynamic-slice_select_fusion.1
  241.9 343.4 %all-reduce.6.cloned.1.call-done = f32[2048,1024]{1,0:T(8,128)} async-done(((f32[2048,1024]{1,0:T(8,128)}), f32[2048,1024]{1,0:T(8,128)}) %all-reduce.6.cloned.1.call-update) | async-done | bytes 8388624 | tf_op jit(solution)/shard_map/psum | solution.py:12
  585.3 0.0 copy-done.3
  585.3 0.0 copy-start.1
  585.3 67.7 %select_add_fusion = f32[1024,2048]{1,0:T(8,128)S(1)} fusion(f32[2048]{0:T(1024)S(1)} %copy-done.3, s32[2048]{0:T(1024)S(1)} %iota_add_fusion, s32[1024]{0:T(1024)S(1)} %iota_add_fusion.1, f32[2048,1024]{1,0:T(8,128)} %all-reduce.6.cloned.1.call-done, f32[2048,2048]{1,0:T(8,128)} %all-gather.2.cloned.1.call-done), kind=kOutput, calls=%fused_computation | convolution fusion | flops 51545899008 | bytes 33574912 | tf_op jit(solution)/shard_map/dot_general | solution.py:29
  653.1 0.0 copy-start.4
  653.1 3.4 copy-done.4
  656.5 0.0 copy-done.1
  656.5 0.0 copy-start.2
  656.5 15.2 %fusion.5 = f32[512,1024]{1,0:T(8,128)} fusion(f32[512,2048]{1,0:T(8,128)S(1)} %copy-done.1, f32[1024,2048]{1,0:T(8,128)S(1)} %select_add_fusion), kind=kOutput, calls=%fused_computation.17 | convolution fusion | flops 12884901888 | bytes 14680064 | tf_op jit(solution)/shard_map/dot_general | solution.py:43
  671.7 0.0 all-reduce.10.cloned.1.call-update
  671.7 0.0 copy-done.2
  671.7 5.8 fusion.4
  677.5 185.2 %all-reduce.10.cloned.1.call-done = (f32[512,1024]{1,0:T(8,128)}, f32[512,1024]{1,0:T(8,128)}) async-done(((f32[512,1024]{1,0:T(8,128)}, f32[512,1024]{1,0:T(8,128)}), (f32[512,1024]{1,0:T(8,128)}, f32[512,1024]{1,0:T(8,128)})) %all-reduce.10.cloned.1.call-update) | async-done | bytes 4194320 | tf_op jit(solution)/shard_map/psum | solution.py:12
  862.7 2.5 multiply_reduce_fusion
  865.2 67.8 %all-reduce = (f32[512]{0:T(512)S(1)}, f32[512]{0:T(512)S(1)}) all-reduce(f32[512]{0:T(512)S(1)} %broadcast_select_fusion.2, f32[512]{0:T(512)S(1)} %broadcast_select_fusion.1), channel_id=1, replica_groups=mesh['row'=16,'col'=8] {'row','col'}, use_global_device_ids=true, to_apply=%region_2.3 | all-reduce | flops 1024 | bytes 8192 | tf_op jit(solution)/shard_map/psum | solution.py:53
  933.0 0.6 sqrt_add_fusion
  (5 shorter events, 0.0 us)
Async XLA Ops:
  7.2 4.4 copy-start
  7.2 99.8 %all-gather.2.cloned.1.call-start = ((), (), s32[]{:S(2)}) async-start(), calls=%async_computation | async-start | bytes 17825792 | tf_op jit(solution)/shard_map/all_gather | solution.py:27
  11.5 227.2 %all-reduce.8.cloned.1.call-start = ((), (), s32[]{:S(2)}) async-start(), calls=%async_computation.2 | async-start | bytes 8388608 | tf_op jit(solution)/shard_map/psum | solution.py:40
  16.1 569.2 %all-reduce.6.cloned.1.call-start = ((), (), s32[]{:S(2)}) async-start(), calls=%async_computation.1 | async-start | bytes 16777216 | tf_op jit(solution)/shard_map/psum | solution.py:12
  115.7 469.7 %copy-start.3 = (f32[2048]{0:T(1024)S(1)}, f32[2048]{0:T(1024)}, u32[]{:S(2)}) copy-start(f32[2048]{0:T(1024)} %param.8) | copy-start | bytes 24580
  115.7 747.0 %all-reduce.10.cloned.1.call-start = ((), (), s32[]{:S(2)}) async-start(), calls=%async_computation.3 | async-start | bytes 8388608 | tf_op jit(solution)/shard_map/psum | solution.py:12
  585.3 71.1 %copy-start.1 = (f32[512,2048]{1,0:T(8,128)S(1)}, f32[512,2048]{1,0:T(8,128)}, u32[]{:S(2)}) copy-start(f32[512,2048]{1,0:T(8,128)} %all-reduce.8.cloned.1.call-done) | copy-start | bytes 12582916
  653.1 3.4 copy-start.4
  656.5 15.3 %copy-start.2 = (f32[2048]{0:T(1024)S(1)}, f32[2048]{0:T(1024)}, u32[]{:S(2)}) copy-start(f32[2048]{0:T(1024)} %param.11) | copy-start | bytes 24580
Sparse Core Ops, SparseCore 0:
  11.7 95.2 all-gather.1
  109.5 129.1 all-reduce.7
  241.8 343.4 all-reduce.5
  671.8 190.8 all-reduce.9
where the time goes:
time: 944 us; the launch traced here: 940 us
  waiting for transfers between devices  742 us (79%)
  matrix products  93.2 us (10%)
  blocking collectives  67.8 us (7%)
  other arithmetic  18 us (2%)
  between operations  14.1 us (1%)
    psum x2, waiting for transfers between devices, spread(): return lax.psum(kept, axis)  529 us
    psum x1, waiting for transfers between devices, body(): cand_col = lax.psum(picked, 'row')  123 us
    all_gather x1, waiting for transfers between devices, body(): col_all = lax.all_gather(masked, 'row', axis=0, tiled=True)  90.8 us
    psum x1, blocking collectives, body(): quad_all, linear_all = lax.psum((quad, linear), ('row', 'col'))  67.8 us
    dot_general x1, matrix products, body(): lax.dot_general(row_all, col_all, contract, precision=high, preferred_ele...  67.7 us
  transfers between devices with their start and end apart: 4, of which 4 were waited for; matrix products, arithmetic and copies ran while one was open for 2% of the time, Pallas kernels for 0%

commit v1 on v0

--- a/solution.py
+++ b/solution.py
@@ -2,6 +2,7 @@
 import jax.numpy as jnp
 from jax import lax
 from jax.sharding import PartitionSpec as P
+from jax.lax import psum
 
 F = 16384
 high = lax.Precision.HIGHEST
@@ -50,7 +51,7 @@
         jnp.dot(cand_col, theta, precision=high, preferred_element_type=jnp.float32),
         jnp.float32(0.0),
     )
-    quad_all, linear_all = lax.psum((quad, linear), ("row", "col"))
+    quad_all, linear_all = psum(psum((quad, linear), axis_name="col"), axis_name="row")
     return (tile, linear_all + jnp.sqrt(quad_all / F))
 
 

time: 944 us -> 914 us (0.968)
  blocking collectives: 67.8 us -> 50.5 us
    psum x1 -> x2, blocking collectives: 67.8 us -> 50.5 us  [the longest x1 31.6 us: body(): psum(psum((quad, linear), axis_name='col'), axis_name='row')]
where the time goes in v1:
time: 914 us
  waiting for transfers between devices  742 us (81%)
  matrix products  84.4 us (9%)
  blocking collectives  50.5 us (6%)
  other arithmetic  18 us (2%)
  between operations  13.9 us (2%)
    psum x2, waiting for transfers between devices, spread(): return lax.psum(kept, axis)  529 us
    psum x1, waiting for transfers between devices, body(): cand_col = lax.psum(picked, 'row')  123 us
    all_gather x1, waiting for transfers between devices, body(): col_all = lax.all_gather(masked, 'row', axis=0, tiled=True)  90.8 us
    dot_general x1, matrix products, body(): lax.dot_general(row_all, col_all, contract, precision=high, preferred_ele...  58.9 us
    psum x1, blocking collectives, body(): psum(psum((quad, linear), axis_name='col'), axis_name='row')  31.6 us
    psum x1, blocking collectives, body(): psum((quad, linear), axis_name='col')  18.9 us
  transfers between devices with their start and end apart: 4, of which 4 were waited for; matrix products, arithmetic and copies ran while one was open for 2% of the time, Pallas kernels for 0%

profile of v1, /device:TPU:1, one launch (start us, length us, event | category | flops | bytes accessed | tf_op | source)
XLA Modules:
  0.0 913.9 jit_solution(10166430245544360324)
XLA Ops:
  7.2 0.0 copy-start
  7.2 0.0 all-gather.2.cloned.1.call-start
  7.2 1.3 dynamic_slice.9
  8.5 0.6 iota_compare_fusion
  9.2 2.3 broadcast_select_fusion
  11.5 0.0 all-gather.2.cloned.1.call-update
  11.5 0.0 all-reduce.9.cloned.1.call-start
  11.6 0.0 copy-done
  11.6 4.5 fusion
  16.1 0.0 all-reduce.9.cloned.1.call-update
  16.1 0.0 all-reduce.7.cloned.1.call-start
  16.2 90.8 %all-gather.2.cloned.1.call-done = f32[2048,2048]{1,0:T(8,128)} async-done(((f32[128,2048]{1,0:T(8,128)}), f32[2048,2048]{1,0:T(8,128)}) %all-gather.2.cloned.1.call-update) | async-done | bytes 16777232 | tf_op jit(solution)/shard_map/all_gather | solution.py:28
  107.0 8.7 dynamic-slice_select_fusion
  115.7 0.0 copy-start.3
  115.7 0.0 all-reduce.7.cloned.1.call-update
  115.7 0.0 all-reduce.11.cloned.1.call-start
  115.8 122.9 %all-reduce.9.cloned.1.call-done = f32[512,2048]{1,0:T(8,128)} async-done(((f32[512,2048]{1,0:T(8,128)}), f32[512,2048]{1,0:T(8,128)}) %all-reduce.9.cloned.1.call-update) | async-done | bytes 4194320 | tf_op jit(solution)/shard_map/psum | solution.py:41
  238.7 3.2 dynamic-slice_select_fusion.1
  241.9 343.4 %all-reduce.7.cloned.1.call-done = f32[2048,1024]{1,0:T(8,128)} async-done(((f32[2048,1024]{1,0:T(8,128)}), f32[2048,1024]{1,0:T(8,128)}) %all-reduce.7.cloned.1.call-update) | async-done | bytes 8388624 | tf_op jit(solution)/shard_map/psum | solution.py:13
  585.3 0.0 copy-done.3
  585.3 0.0 copy-start.1
  585.3 58.9 %select_add_fusion = f32[1024,2048]{1,0:T(8,128)S(1)} fusion(f32[2048]{0:T(1024)S(1)} %copy-done.3, s32[2048]{0:T(1024)S(1)} %iota_add_fusion, s32[1024]{0:T(1024)S(1)} %iota_add_fusion.1, f32[2048,1024]{1,0:T(8,128)} %all-reduce.7.cloned.1.call-done, f32[2048,2048]{1,0:T(8,128)} %all-gather.2.cloned.1.call-done), kind=kOutput, calls=%fused_computation | convolution fusion | flops 51545899008 | bytes 33574912 | tf_op jit(solution)/shard_map/dot_general | solution.py:30
  644.2 0.0 copy-start.4
  644.2 3.4 copy-done.4
  647.6 0.0 copy-done.1
  647.6 0.0 copy-start.2
  647.6 15.3 %fusion.5 = f32[512,1024]{1,0:T(8,128)} fusion(f32[512,2048]{1,0:T(8,128)S(1)} %copy-done.1, f32[1024,2048]{1,0:T(8,128)S(1)} %select_add_fusion), kind=kOutput, calls=%fused_computation.17 | convolution fusion | flops 12884901888 | bytes 14680064 | tf_op jit(solution)/shard_map/dot_general | solution.py:44
  662.9 0.0 all-reduce.11.cloned.1.call-update
  662.9 0.0 copy-done.2
  662.9 5.8 fusion.4
  668.7 185.1 %all-reduce.11.cloned.1.call-done = (f32[512,1024]{1,0:T(8,128)}, f32[512,1024]{1,0:T(8,128)}) async-done(((f32[512,1024]{1,0:T(8,128)}, f32[512,1024]{1,0:T(8,128)}), (f32[512,1024]{1,0:T(8,128)}, f32[512,1024]{1,0:T(8,128)})) %all-reduce.11.cloned.1.call-update) | async-done | bytes 4194320 | tf_op jit(solution)/shard_map/psum | solution.py:13
  853.8 2.5 multiply_reduce_fusion
  856.3 18.9 %all-reduce.1 = (f32[512]{0:T(512)S(1)}, f32[512]{0:T(512)S(1)}) all-reduce(f32[512]{0:T(512)S(1)} %broadcast_select_fusion.2, f32[512]{0:T(512)S(1)} %broadcast_select_fusion.1), channel_id=1, replica_groups=mesh['row'=16,'col'=8] {'col'}, use_global_device_ids=true, to_apply=%region_2.3 | all-reduce | flops 1024 | bytes 8192 | tf_op jit(solution)/shard_map/psum | solution.py:54
  875.2 31.6 %all-reduce = (f32[512]{0:T(512)S(1)}, f32[512]{0:T(512)S(1)}) all-reduce(f32[512]{0:T(512)S(1)} %get-tuple-element.4, f32[512]{0:T(512)S(1)} %get-tuple-element.5), channel_id=1, replica_groups=mesh['row'=16,'col'=8] {'row'}, use_global_device_ids=true, to_apply=%region_3.4 | all-reduce | flops 1024 | bytes 8192 | tf_op jit(solution)/shard_map/psum | solution.py:54
  906.8 0.6 sqrt_add_fusion
  (5 shorter events, 0.0 us)
Async XLA Ops:
  7.2 4.4 copy-start
  7.2 99.8 %all-gather.2.cloned.1.call-start = ((), (), s32[]{:S(2)}) async-start(), calls=%async_computation | async-start | bytes 17825792 | tf_op jit(solution)/shard_map/all_gather | solution.py:28
  11.5 227.2 %all-reduce.9.cloned.1.call-start = ((), (), s32[]{:S(2)}) async-start(), calls=%async_computation.2 | async-start | bytes 8388608 | tf_op jit(solution)/shard_map/psum | solution.py:41
  16.1 569.2 %all-reduce.7.cloned.1.call-start = ((), (), s32[]{:S(2)}) async-start(), calls=%async_computation.1 | async-start | bytes 16777216 | tf_op jit(solution)/shard_map/psum | solution.py:13
  115.7 469.7 %copy-start.3 = (f32[2048]{0:T(1024)S(1)}, f32[2048]{0:T(1024)}, u32[]{:S(2)}) copy-start(f32[2048]{0:T(1024)} %param.8) | copy-start | bytes 24580
  115.7 738.2 %all-reduce.11.cloned.1.call-start = ((), (), s32[]{:S(2)}) async-start(), calls=%async_computation.3 | async-start | bytes 8388608 | tf_op jit(solution)/shard_map/psum | solution.py:13
  585.3 62.3 %copy-start.1 = (f32[512,2048]{1,0:T(8,128)S(1)}, f32[512,2048]{1,0:T(8,128)}, u32[]{:S(2)}) copy-start(f32[512,2048]{1,0:T(8,128)} %all-reduce.9.cloned.1.call-done) | copy-start | bytes 12582916
  644.2 3.4 copy-start.4
  647.6 15.3 %copy-start.2 = (f32[2048]{0:T(1024)S(1)}, f32[2048]{0:T(1024)}, u32[]{:S(2)}) copy-start(f32[2048]{0:T(1024)} %param.11) | copy-start | bytes 24580
Sparse Core Ops, SparseCore 0:
  11.7 95.2 all-gather.1
  109.5 129.1 all-reduce.8
  241.8 343.4 all-reduce.6
  663.0 190.7 all-reduce.10
